TPU v7x, 256 devices: a whole 4x4x8 slice. The times are simulated.
256 devices in a mesh: dp: 32 (over x_lo, z, core), blk: 8 (over y, x_hi).
Axes of the slice: x: 4 (x_hi: 2, x_lo: 2; x = x_hi * 2 + x_lo), y: 4, z: 8, core: 2. Of those that a mesh axis runs over, the one named last changes fastest.
Arguments:
- inputs: bfloat16 [8, 16384, 4096], P('blk', 'dp'), may hold values from -6 to 6
- out_grads: bfloat16 [8, 16384, 4096], P('blk', 'dp'), may hold values from -8 to 8
- test_matrix: bfloat16 [8, 4096, 256], P('blk'), may hold values from -6 to 6
- momentum: bfloat16 [8, 4096, 4096], P(None, 'blk', 'dp'), may hold values from -6 to 6
Outputs:
- update: bfloat16 [8, 4096, 4096], P(None, 'blk', 'dp')
All inputs are finite; a program needn't handle non-finite values.
Results may differ from a plain program's by a relative error of at most 0.0035.
Values may be sent and summed in bfloat16 or wider, within the bound.
No kernel may reach another device: no remote copies, remote signals or barrier semaphores. Data moves between devices by JAX's collectives and lax.ppermute only.
A program may use at most 128 MiB of HBM per device.

v0:
```python
import jax
import jax.numpy as jnp
from jax import lax
from jax.sharding import PartitionSpec as P


def inner_gram(columns):
    return lax.dot_general(
        columns, columns, (((0,), (0,)), ((), ())), precision=lax.Precision.HIGHEST
    )


def cholesky_pass(columns, gram_matrix):
    lower_factor = jnp.linalg.cholesky(gram_matrix)
    return lax.linalg.triangular_solve(
        lower_factor, columns, left_side=False, lower=True, transpose_a=True
    )


def shards(inputs, out_grads, test_matrix, momentum):
    features = inputs[0]
    errors = out_grads[0]
    probes = test_matrix[0]
    replicas = lax.axis_size("dp")
    scale = 1.0 / (features.shape[1] * features.shape[0] * replicas)
    columns = lax.all_to_all(momentum, "blk", split_axis=0, concat_axis=1, tiled=True)[0]
    projected = jnp.dot(features, probes, preferred_element_type=jnp.float32).astype(jnp.bfloat16)
    token_gram = lax.dot_general(
        errors, errors, (((1,), (1,)), ((), ())), preferred_element_type=jnp.float32
    ).astype(jnp.bfloat16)
    mixed_rows = jnp.dot(token_gram, projected, preferred_element_type=jnp.float32).astype(
        jnp.bfloat16
    )
    sketch_term = (
        lax.dot_general(
            features, mixed_rows, (((0,), (0,)), ((), ())), preferred_element_type=jnp.float32
        )
        * scale
    )
    sketch = lax.psum(sketch_term, "dp")
    basis = cholesky_pass(sketch, inner_gram(sketch)).astype(jnp.bfloat16)
    reduced = jnp.dot(features, basis, preferred_element_type=jnp.float32).astype(jnp.bfloat16)
    shaped = jnp.dot(token_gram, reduced, preferred_element_type=jnp.float32).astype(jnp.bfloat16)
    core_term = (
        lax.dot_general(
            reduced, shaped, (((0,), (0,)), ((), ())), preferred_element_type=jnp.float32
        )
        * scale
    )
    core_matrix = lax.psum(core_term, "dp")
    shifted = core_matrix + jnp.eye(core_matrix.shape[0], dtype=jnp.float32)
    lower_factor = jnp.linalg.cholesky(shifted)
    half_solved = lax.linalg.triangular_solve(lower_factor, core_matrix, left_side=True, lower=True)
    factor = lax.linalg.triangular_solve(
        lower_factor, half_solved, left_side=True, lower=True, transpose_a=True
    )
    coeffs = lax.dot_general(
        basis, columns, (((0,), (0,)), ((), ())), preferred_element_type=jnp.float32
    )
    scaled = jnp.dot(factor, coeffs, precision=lax.Precision.HIGHEST).astype(jnp.bfloat16)
    fresh = (
        columns.astype(jnp.float32) - jnp.dot(basis, scaled, preferred_element_type=jnp.float32)
    ).astype(jnp.bfloat16)
    return lax.all_to_all(fresh[None], "blk", split_axis=1, concat_axis=0, tiled=True)


def solution(mesh):
    in_specs = (
        P("blk", "dp", None),
        P("blk", "dp", None),
        P("blk", None, None),
        P(None, "blk", "dp"),
    )
    out_specs = P(None, "blk", "dp")
    return jax.shard_map(shards, mesh=mesh, in_specs=in_specs, out_specs=out_specs, check_vma=False)
```

profile of v0, /device:TPU:1, one launch (start us, length us, event | category | flops | bytes accessed | tf_op | source)
XLA Modules:
  0.0 706.3 jit_solution(12601974615667945552)
XLA Ops:
  6.5 6.0 fusion.13
  12.5 1.3 fusion.16
  13.8 5.9 fusion
  19.7 7.5 %all-to-all-start = ((bf16[8,512,128]{2,1,0:T(8,128)(2,1)}), bf16[8,512,128]{2,1,0:T(8,128)(2,1)}, u32[]{:S(2)}, u32[]{:S(2)}) async-start(bf16[8,512,128]{2,1,0:T(8,128)(2,1)} %param.8), calls=%async_computation | async-start | bytes 2097152 | tf_op jit(solution)/shard_map/all_to_all | solution.py:26
  27.3 231.4 %all-reduce.4.cloned.1.call-done = f32[4096,256]{0,1:T(8,128)} async-done(((f32[4096,256]{0,1:T(8,128)}), f32[4096,256]{0,1:T(8,128)}) %all-reduce.4.cloned.1.call-update) | async-done | bytes 4194320 | tf_op jit(solution)/shard_map/psum | solution.py:40
  258.7 12.1 %fusion.53 = f32[256,256]{1,0:T(8,128)S(1)} fusion(f32[4096,256]{0,1:T(8,128)} %all-reduce.4.cloned.1.call-done), kind=kOutput, calls=%fused_computation.90 | convolution fusion | flops 3221225472 | bytes 4456448 | tf_op jit(solution)/shard_map/dot_general | solution.py:8
  271.0 11.7 %cholesky.130 = f32[128,128]{1,0:T(8,128)S(1)} custom-call(f32[128,128]{1,0:T(8,128)S(1)} %cholesky.194), custom_call_target="Cholesky" | custom-call | tf_op jit(solution)/shard_map/jit(cholesky)/cholesky | solution.py:14
  282.8 9.8 %custom-call.19 = f32[1,128,128]{1,2,0:T(8,128)S(1)} custom-call(f32[1,128,128]{2,1,0:T(8,128)S(1)} %get-tuple-element.49), custom_call_target="InvertDiagBlocksLowerTriangular" | custom-call | tf_op jit(solution)/shard_map/jit(cholesky)/cholesky | solution.py:14
  293.1 11.7 %cholesky.147 = f32[128,128]{1,0:T(8,128)S(1)} custom-call(f32[128,128]{1,0:T(8,128)S(1)} %convolution_subtract_fusion.5), custom_call_target="Cholesky" | custom-call | tf_op jit(solution)/shard_map/jit(cholesky)/cholesky | solution.py:14
  304.8 0.7 compare_reduce_fusion.2
  306.9 3.9 while.2
  306.9 0.6 fusion.77
  307.5 1.3 bitcast_dynamic-update-slice_fusion.4
  308.8 0.6 fusion.77
  309.4 1.3 bitcast_dynamic-update-slice_fusion.4
  310.8 19.9 %custom-call.16 = f32[2,128,128]{1,2,0:T(8,128)S(1)} custom-call(f32[2,128,128]{2,1,0:T(8,128)S(1)} %get-tuple-element.13), custom_call_target="InvertDiagBlocksLowerTriangular" | custom-call | tf_op jit(solution)/shard_map/triangular_solve | solution.py:15
  330.7 3.7 fusion.52
  334.4 2.0 convolution_subtract_fusion.1
  336.5 2.0 convolution_convert_fusion
  338.5 1.0 copy-done.5
  339.4 1.3 fusion.21
  340.7 1.3 fusion.25
  342.1 2.6 fusion.26
  344.7 216.2 %all-reduce.6.cloned.1.call-done = f32[256,256]{0,1:T(8,128)} async-done(((f32[256,256]{0,1:T(8,128)}), f32[256,256]{0,1:T(8,128)}) %all-reduce.6.cloned.1.call-update) | async-done | bytes 262160 | tf_op jit(solution)/shard_map/psum | solution.py:50
  560.9 1.0 convert_add_fusion
  562.1 1.0 fusion.30
  563.1 12.1 %cholesky.164 = f32[128,128]{1,0:T(8,128)S(1)} custom-call(f32[128,128]{1,0:T(8,128)S(1)} %cholesky.197), custom_call_target="Cholesky" | custom-call | tf_op jit(solution)/shard_map/jit(cholesky)/cholesky | solution.py:52
  575.3 9.8 %custom-call.20 = f32[1,128,128]{1,2,0:T(8,128)S(1)} custom-call(f32[1,128,128]{2,1,0:T(8,128)S(1)} %get-tuple-element.45), custom_call_target="InvertDiagBlocksLowerTriangular" | custom-call | tf_op jit(solution)/shard_map/jit(cholesky)/cholesky | solution.py:52
  585.5 11.7 %cholesky.181 = f32[128,128]{1,0:T(8,128)S(1)} custom-call(f32[128,128]{1,0:T(8,128)S(1)} %convolution_subtract_fusion.4), custom_call_target="Cholesky" | custom-call | tf_op jit(solution)/shard_map/jit(cholesky)/cholesky | solution.py:52
  597.3 0.7 compare_reduce_fusion
  598.0 0.6 compare_reduce_fusion.1
  599.9 3.8 while.3
  599.9 0.6 fusion.78
  600.5 1.3 bitcast_dynamic-update-slice_fusion.5
  601.8 0.6 fusion.78
  602.4 1.3 bitcast_dynamic-update-slice_fusion.5
  603.7 19.7 %custom-call.17 = f32[2,128,128]{1,2,0:T(8,128)S(1)} custom-call(f32[2,128,128]{2,1,0:T(8,128)S(1)} %get-tuple-element.21), custom_call_target="InvertDiagBlocksLowerTriangular" | custom-call | tf_op jit(solution)/shard_map/triangular_solve | solution.py:54
  623.7 0.4 convolution_subtract_fusion.3
  624.1 0.3 fusion.43
  625.3 0.4 convolution_convert_fusion.3
  625.7 2.7 fusion.2
  628.4 17.2 %copy.23 = bf16[1,4096,128]{2,0,1:T(2,128)(2,1)} copy(bf16[1,4096,128]{2,1,0:T(8,128)(2,1)S(1)} %fusion.2) | data formatting | bytes 2097152 | tf_op jit(solution)/shard_map/broadcast_in_dim | solution.py:64
  645.6 0.5 broadcast.127
  646.1 23.4 %reduce.8 = bf16[4096,128]{1,0:T(8,128)(2,1)S(1)} reduce(bf16[4096,1,128]{2,1,0:T(2,128)(2,1)} %bitcast.111, bf16[]{:T(256)} %broadcast.127), dimensions={1}, to_apply=%bitcast.97.reduce_sub_computation | reduce | bytes 2097154
  669.5 1.1 reshape.68
  670.6 22.5 %all_to_all.21 = bf16[8,2,32768]{2,1,0:T(2,128)(2,1)S(1)} all-to-all(bf16[8,2,32768]{2,1,0:T(2,128)(2,1)} %reshape.68), channel_id=1, replica_groups=mesh['dp'=32,'blk'=8] {'blk'}, dimensions={0} | all-to-all | bytes 2097152 | tf_op jit(solution)/shard_map/all_to_all | solution.py:64
  693.1 3.5 reshape.69
  696.6 2.7 copy.21
  (47 shorter events, 2.9 us)
Async XLA Ops:
  6.5 6.0 copy-start
  6.5 252.2 %all-reduce.4.cloned.1.call-start = ((), (), s32[]{:S(2)}) async-start(), calls=%async_computation.2 | async-start | bytes 8388608 | tf_op jit(solution)/shard_map/psum | solution.py:40
  6.5 6.0 copy-start.2
  19.7 322.3 %all-to-all-start = ((bf16[8,512,128]{2,1,0:T(8,128)(2,1)}), bf16[8,512,128]{2,1,0:T(8,128)(2,1)}, u32[]{:S(2)}, u32[]{:S(2)}) async-start(bf16[8,512,128]{2,1,0:T(8,128)(2,1)} %param.8), calls=%async_computation | async-start | bytes 2097152 | tf_op jit(solution)/shard_map/all_to_all | solution.py:26
  27.3 533.6 %all-reduce.6.cloned.1.call-start = ((), (), s32[]{:S(2)}) async-start(), calls=%async_computation.3 | async-start | bytes 524288 | tf_op jit(solution)/shard_map/psum | solution.py:50
  330.6 3.8 copy-start.1
  334.4 4.1 copy-start.6
  334.4 5.0 copy-start.3
  338.5 1.0 copy-start.5
  560.9 62.5 %copy-start.4 = (f32[256,256]{0,1:T(8,128)S(1)}, f32[256,256]{0,1:T(8,128)}, u32[]{:S(2)}) copy-start(f32[256,256]{0,1:T(8,128)} %all-reduce.6.cloned.1.call-done) | copy-start | bytes 786436
Sparse Core Ops, SparseCore 0:
  19.9 238.8 all-reduce.3
  342.2 218.6 all-reduce.5
where the time goes:
time: 713 us; the launch traced here: 706 us
  waiting for transfers between devices  448 us (63%)
  other arithmetic  134 us (19%)
  matrix products  44 us (6%)
  local copies, waits for them, and re-layouts  34 us (5%)
  blocking collectives  22.5 us (3%)
  between operations  16.4 us (2%)
  starting transfers between devices  7.55 us (1%)
    psum x1, waiting for transfers between devices, shards(): sketch = lax.psum(sketch_term, 'dp')  231 us
    psum x1, waiting for transfers between devices, shards(): core_matrix = lax.psum(core_term, 'dp')  216 us
    another operation x7, other arithmetic, shards(): lower_factor = jnp.linalg.cholesky(shifted)  35 us
    another operation x6, other arithmetic, cholesky_pass(): lower_factor = jnp.linalg.cholesky(gram_matrix)  34 us
    unnamed x1, other arithmetic  23.4 us
    all_to_all x1, blocking collectives, shards(): lax.all_to_all(fresh[None], 'blk', split_axis=1, concat_axis=0, tiled=True)  22.5 us
    another operation x3, other arithmetic, cholesky_pass(): lax.linalg.triangular_solve(lower_factor, columns, left_side=False, lower...  19.9 us
    another operation x2, other arithmetic, shards(): lax.linalg.triangular_solve(lower_factor, half_solved, left_side=True, lo...  19.7 us
  transfers between devices with their start and end apart: 3, of which 2 were waited for; matrix products, arithmetic and copies ran while one was open for 12% of the time, Pallas kernels for 0%

commit v1 on v0

--- a/solution.py
+++ b/solution.py
@@ -2,6 +2,19 @@
 import jax.numpy as jnp
 from jax import lax
 from jax.sharding import PartitionSpec as P
+
+
+def _make_records(base_x, out_dim, dimension_no):
+    seen_now = jnp.concatenate(
+        lax.all_to_all(
+            jnp.stack(jnp.split(base_x, lax.psum(1, "blk"), axis=out_dim)),
+            axis_name="blk",
+            split_axis=0,
+            concat_axis=0,
+        ),
+        axis=dimension_no,
+    )
+    return seen_now
 
 
 def inner_gram(columns):
@@ -61,7 +74,7 @@
     fresh = (
         columns.astype(jnp.float32) - jnp.dot(basis, scaled, preferred_element_type=jnp.float32)
     ).astype(jnp.bfloat16)
-    return lax.all_to_all(fresh[None], "blk", split_axis=1, concat_axis=0, tiled=True)
+    return _make_records(fresh[None], 1, 0)
 
 
 def solution(mesh):

time: 713 us -> 665 us (0.933)
  other arithmetic: 134 us -> 110 us
  local copies, waits for them, and re-layouts: 34 us -> 10.1 us
    unnamed x1 -> x0, other arithmetic: 23.4 us -> none
    broadcast_in_dim x1 -> x0, local copies, waits for them, and re-layouts: 17.2 us -> none  [shards(): fresh[None]]
  transfers between devices with their start and end apart: 3 -> 3, of which waited for: 2 -> 2; matrix products, arithmetic and copies ran while one was open for 12% -> 13% of each run, Pallas kernels for 0% -> 0%
where the time goes in v1:
time: 665 us; the launch traced here: 659 us
  waiting for transfers between devices  448 us (67%)
  other arithmetic  110 us (17%)
  matrix products  44.2 us (7%)
  blocking collectives  22.3 us (3%)
  between operations  16.5 us (2%)
  local copies, waits for them, and re-layouts  10.1 us (2%)
  starting transfers between devices  7.56 us (1%)
    psum x1, waiting for transfers between devices, shards(): sketch = lax.psum(sketch_term, 'dp')  231 us
    psum x1, waiting for transfers between devices, shards(): core_matrix = lax.psum(core_term, 'dp')  216 us
    another operation x7, other arithmetic, shards(): lower_factor = jnp.linalg.cholesky(shifted)  34.8 us
    another operation x6, other arithmetic, cholesky_pass(): lower_factor = jnp.linalg.cholesky(gram_matrix)  34 us
    all_to_all x1, blocking collectives, _make_records(): lax.all_to_all(jnp.stack(jnp.split(base_x, lax.psum(1, 'blk'), axis=out_d...  22.3 us
    another operation x3, other arithmetic, cholesky_pass(): lax.linalg.triangular_solve(lower_factor, columns, left_side=False, lower...  19.9 us
    another operation x2, other arithmetic, shards(): lax.linalg.triangular_solve(lower_factor, half_solved, left_side=True, lo...  19.7 us
  transfers between devices with their start and end apart: 3, of which 2 were waited for; matrix products, arithmetic and copies ran while one was open for 13% of the time, Pallas kernels for 0%

profile of v1, /device:TPU:1, one launch (start us, length us, event | category | flops | bytes accessed | tf_op | source)
XLA Modules:
  0.0 658.9 jit_solution(8992191758235351324)
XLA Ops:
  6.5 6.0 fusion.13
  12.5 1.3 fusion.16
  13.8 5.9 fusion
  19.7 7.5 %all-to-all-start = ((bf16[8,512,128]{2,1,0:T(8,128)(2,1)}), bf16[8,512,128]{2,1,0:T(8,128)(2,1)}, u32[]{:S(2)}, u32[]{:S(2)}) async-start(bf16[8,512,128]{2,1,0:T(8,128)(2,1)} %param.8), calls=%async_computation | async-start | bytes 2097152 | tf_op jit(solution)/shard_map/all_to_all | solution.py:39
  27.3 231.4 %all-reduce.4.cloned.1.call-done = f32[4096,256]{0,1:T(8,128)} async-done(((f32[4096,256]{0,1:T(8,128)}), f32[4096,256]{0,1:T(8,128)}) %all-reduce.4.cloned.1.call-update) | async-done | bytes 4194320 | tf_op jit(solution)/shard_map/psum | solution.py:53
  258.7 12.4 %fusion.61 = f32[256,256]{1,0:T(8,128)S(1)} fusion(f32[4096,256]{0,1:T(8,128)} %all-reduce.4.cloned.1.call-done), kind=kOutput, calls=%fused_computation.105 | convolution fusion | flops 3221225472 | bytes 4456448 | tf_op jit(solution)/shard_map/dot_general | solution.py:21
  271.3 11.7 %cholesky.130 = f32[128,128]{1,0:T(8,128)S(1)} custom-call(f32[128,128]{1,0:T(8,128)S(1)} %cholesky.194), custom_call_target="Cholesky" | custom-call | tf_op jit(solution)/shard_map/jit(cholesky)/cholesky | solution.py:27
  283.1 9.8 %custom-call.19 = f32[1,128,128]{1,2,0:T(8,128)S(1)} custom-call(f32[1,128,128]{2,1,0:T(8,128)S(1)} %get-tuple-element.49), custom_call_target="InvertDiagBlocksLowerTriangular" | custom-call | tf_op jit(solution)/shard_map/jit(cholesky)/cholesky | solution.py:27
  293.1 0.3 convolution_subtract_fusion.5
  293.4 11.7 %cholesky.147 = f32[128,128]{1,0:T(8,128)S(1)} custom-call(f32[128,128]{1,0:T(8,128)S(1)} %convolution_subtract_fusion.5), custom_call_target="Cholesky" | custom-call | tf_op jit(solution)/shard_map/jit(cholesky)/cholesky | solution.py:27
  305.2 0.7 compare_reduce_fusion.2
  307.2 3.9 while.2
  307.2 0.6 fusion.85
  307.8 1.3 bitcast_dynamic-update-slice_fusion.4
  309.1 0.6 fusion.85
  309.7 1.3 bitcast_dynamic-update-slice_fusion.4
  311.1 19.8 %custom-call.16 = f32[2,128,128]{1,2,0:T(8,128)S(1)} custom-call(f32[2,128,128]{2,1,0:T(8,128)S(1)} %get-tuple-element.13), custom_call_target="InvertDiagBlocksLowerTriangular" | custom-call | tf_op jit(solution)/shard_map/triangular_solve | solution.py:28
  330.9 3.7 fusion.60
  334.7 2.0 convolution_subtract_fusion.1
  336.7 2.0 convolution_convert_fusion
  338.7 1.0 copy-done.5
  339.7 1.3 fusion.21
  341.0 1.3 fusion.25
  342.4 2.5 fusion.26
  344.9 216.3 %all-reduce.6.cloned.1.call-done = f32[256,256]{0,1:T(8,128)} async-done(((f32[256,256]{0,1:T(8,128)}), f32[256,256]{0,1:T(8,128)}) %all-reduce.6.cloned.1.call-update) | async-done | bytes 262160 | tf_op jit(solution)/shard_map/psum | solution.py:63
  561.2 1.0 convert_add_fusion
  562.4 1.0 fusion.30
  563.4 11.9 %cholesky.164 = f32[128,128]{1,0:T(8,128)S(1)} custom-call(f32[128,128]{1,0:T(8,128)S(1)} %cholesky.197), custom_call_target="Cholesky" | custom-call | tf_op jit(solution)/shard_map/jit(cholesky)/cholesky | solution.py:65
  575.3 9.8 %custom-call.20 = f32[1,128,128]{1,2,0:T(8,128)S(1)} custom-call(f32[1,128,128]{2,1,0:T(8,128)S(1)} %get-tuple-element.45), custom_call_target="InvertDiagBlocksLowerTriangular" | custom-call | tf_op jit(solution)/shard_map/jit(cholesky)/cholesky | solution.py:65
  585.4 0.3 convolution_subtract_fusion.4
  585.6 11.7 %cholesky.181 = f32[128,128]{1,0:T(8,128)S(1)} custom-call(f32[128,128]{1,0:T(8,128)S(1)} %convolution_subtract_fusion.4), custom_call_target="Cholesky" | custom-call | tf_op jit(solution)/shard_map/jit(cholesky)/cholesky | solution.py:65
  597.4 0.7 compare_reduce_fusion
  598.1 0.6 compare_reduce_fusion.1
  600.0 3.8 while.3
  600.0 0.6 fusion.86
  600.6 1.3 bitcast_dynamic-update-slice_fusion.5
  601.9 0.6 fusion.86
  602.5 1.3 bitcast_dynamic-update-slice_fusion.5
  603.8 19.7 %custom-call.17 = f32[2,128,128]{1,2,0:T(8,128)S(1)} custom-call(f32[2,128,128]{2,1,0:T(8,128)S(1)} %get-tuple-element.21), custom_call_target="InvertDiagBlocksLowerTriangular" | custom-call | tf_op jit(solution)/shard_map/triangular_solve | solution.py:67
  623.5 0.3 fusion.40
  623.8 0.4 convolution_subtract_fusion.3
  624.2 0.3 fusion.51
  624.8 0.3 convolution_subtract_fusion.2
  625.1 0.3 fusion.49
  625.4 0.4 convolution_convert_fusion.3
  625.8 2.6 fusion.2
  628.6 22.3 %all_to_all.14 = bf16[8,1,512,128]{3,2,1,0:T(8,128)(2,1)S(1)} all-to-all(bf16[8,1,512,128]{3,2,1,0:T(8,128)(2,1)S(1)} %fusion.32), channel_id=1, replica_groups=mesh['dp'=32,'blk'=8] {'blk'}, dimensions={0} | all-to-all | bytes 2097152 | tf_op jit(solution)/shard_map/all_to_all | solution.py:9
  650.9 1.0 copy.41
  (50 shorter events, 1.6 us)
Async XLA Ops:
  6.5 6.0 copy-start
  6.5 252.2 %all-reduce.4.cloned.1.call-start = ((), (), s32[]{:S(2)}) async-start(), calls=%async_computation.2 | async-start | bytes 8388608 | tf_op jit(solution)/shard_map/psum | solution.py:53
  6.5 6.0 copy-start.2
  19.7 322.6 %all-to-all-start = ((bf16[8,512,128]{2,1,0:T(8,128)(2,1)}), bf16[8,512,128]{2,1,0:T(8,128)(2,1)}, u32[]{:S(2)}, u32[]{:S(2)}) async-start(bf16[8,512,128]{2,1,0:T(8,128)(2,1)} %param.8), calls=%async_computation | async-start | bytes 2097152 | tf_op jit(solution)/shard_map/all_to_all | solution.py:39
  27.3 533.9 %all-reduce.6.cloned.1.call-start = ((), (), s32[]{:S(2)}) async-start(), calls=%async_computation.3 | async-start | bytes 524288 | tf_op jit(solution)/shard_map/psum | solution.py:63
  330.9 3.8 copy-start.1
  334.7 4.1 copy-start.6
  334.7 5.0 copy-start.3
  338.7 1.0 copy-start.5
  561.2 62.3 %copy-start.4 = (f32[256,256]{0,1:T(8,128)S(1)}, f32[256,256]{0,1:T(8,128)}, u32[]{:S(2)}) copy-start(f32[256,256]{0,1:T(8,128)} %all-reduce.6.cloned.1.call-done) | copy-start | bytes 786436
Sparse Core Ops, SparseCore 0:
  19.9 238.8 all-reduce.3
  342.5 218.6 all-reduce.5
